TPU v7x, 32 devices: a whole 2x2x4 slice. The times are simulated.
32 devices in a mesh: groups: 2 (over x), seq: 8 (over z, y), chan: 2 (over core).
Axes of the slice: x: 2, y: 2, z: 4, core: 2. Of those that a mesh axis runs over, the one named last changes fastest.
Arguments:
- cached_input: bfloat16 [2048, 4096], P(('groups', 'seq'), 'chan'), parts along dimension 0, may hold values from -6 to 6
- cached_gate: bfloat16 [2048, 4096], P(('groups', 'seq'), 'chan'), parts along dimension 0, may hold values from -6 to 6
- out_grad: bfloat16 [2048, 4096], P(('groups', 'seq'), 'chan'), parts along dimension 0, may hold values from -1.75 to 1.75
- filter_taps: bfloat16 [1024, 32], P('seq', 'chan'), may hold values from -6 to 6
- skip_gain: float32 [4096], P('chan'), may hold values from -1 to 1
Outputs:
- input_grad: bfloat16 [2048, 4096], P(('groups', 'seq'), 'chan'), parts along dimension 0
- filter_grad: float32 [2048, 32], P(('groups', 'seq'), 'chan'), parts along dimension 0
There are 2 independent parts, one for each index of `groups`. A program takes and returns all parts, laid end to end along the dimension named above; an argument that names none is the same for every part. Nothing has to cross between parts.
All inputs are finite; a program needn't handle non-finite values.
Results may differ from a plain program's by a relative error of at most 0.005.
Values may be sent and summed in bfloat16 or wider, within the bound.
No kernel may reach another device: no remote copies, remote signals or barrier semaphores. Data moves between devices by JAX's collectives and lax.ppermute only.
A program may use at most 64 MiB of HBM per device.

v0:
```python
import math
import jax
import numpy as np
import jax.numpy as jnp
from jax import lax
from jax.sharding import PartitionSpec as P

lag_group = 4


def toeplitz_blocks(windows, block_rows):
    flipped = windows[..., ::-1]
    tiled = jnp.tile(flipped, (1, 1, block_rows))
    trimmed = tiled[..., : block_rows * (2 * block_rows - 1)]
    shaped = trimmed.reshape(windows.shape[0], windows.shape[1], block_rows, 2 * block_rows - 1)
    return shaped[..., block_rows - 1 : 2 * block_rows - 1]


def diagonal_sums(products, block_rows):
    flipped = products[..., ::-1]
    padded = jnp.pad(flipped, ((0, 0), (0, 0), (0, 0), (0, block_rows)))
    flattened = padded.reshape(products.shape[0], products.shape[1], 2 * block_rows * block_rows)
    trimmed = flattened[..., : block_rows * (2 * block_rows - 1)]
    shaped = trimmed.reshape(products.shape[0], products.shape[1], block_rows, 2 * block_rows - 1)
    diag_sums = jnp.sum(shaped, axis=2)
    return jnp.pad(diag_sums, ((0, 0), (0, 0), (1, 0)))


def fold_windows(window_grads, block_rows):
    front_half = jnp.pad(window_grads[..., :block_rows], ((0, 1), (0, 0), (0, 0)))
    back_half = jnp.pad(window_grads[..., block_rows:], ((1, 0), (0, 0), (0, 0)))
    joined = front_half + back_half
    return jnp.transpose(joined, (1, 0, 2)).reshape(window_grads.shape[1], -1)


def lag_table(taps_all, block_rows):
    return jnp.pad(jnp.transpose(taps_all), ((0, 0), (block_rows, lag_group * block_rows)))


def lag_sweep(
    blocks, base_block, block_count, sources, tap_table, block_rows, trip_count, seq_count
):
    filters = sources.shape[2]
    group_width = sources.shape[3]

    def advance(lag_step, state_pair):
        input_acc, lag_acc = state_pair
        lag_start = lag_step * lag_group
        stacked = jnp.stack(
            [
                lax.dynamic_slice_in_dim(blocks, base_block + lag_start + offset, block_count, 0)
                for offset in range(lag_group)
            ],
            axis=1,
        )
        lag_span = lax.dynamic_slice_in_dim(
            tap_table, lag_start * block_rows, (lag_group + 1) * block_rows, 1
        )
        windows = jnp.stack(
            [
                lag_span[:, offset * block_rows : (offset + 2) * block_rows]
                for offset in range(lag_group)
            ],
            axis=0,
        )
        toeplitz = toeplitz_blocks(windows, block_rows)
        input_acc = input_acc + jnp.einsum(
            "kfts,iktfg->isfg", toeplitz, stacked, preferred_element_type=jnp.float32
        )
        products = jnp.einsum(
            "iktfg,isfg->kfts", stacked, sources, preferred_element_type=jnp.float32
        )
        folded = fold_windows(diagonal_sums(products, block_rows), block_rows)
        previous = lax.dynamic_slice_in_dim(
            lag_acc, lag_start * block_rows, (lag_group + 1) * block_rows, 1
        )
        lag_acc = lax.dynamic_update_slice_in_dim(
            lag_acc, previous + folded, lag_start * block_rows, 1
        )
        return (input_acc, lag_acc)

    initial = (
        jnp.zeros((block_count, block_rows, filters, group_width), jnp.float32),
        jnp.zeros((filters, (seq_count + 1 + lag_group) * block_rows), jnp.float32),
    )
    return lax.fori_loop(0, trip_count, advance, initial)


def per_device(cached_input, cached_gate, out_grad, filter_taps, skip_gain):
    block_rows = cached_input.shape[0]
    chan_width = cached_input.shape[1]
    filters = filter_taps.shape[1]
    group_width = chan_width // filters
    seq_count = lax.axis_size("seq")
    seq_index = lax.axis_index("seq")
    length = block_rows * seq_count
    taps_scale = 1.0 / math.sqrt(length)
    gated_grad = (out_grad.astype(jnp.float32) * cached_gate.astype(jnp.float32)).astype(
        jnp.bfloat16
    )
    stretch_width = chan_width // seq_count
    stretch_filters = max(1, stretch_width // group_width)
    stretch_group = stretch_width // stretch_filters
    first_filter = seq_index * stretch_width // group_width
    tap_columns = np.array(
        [
            target * stretch_width // group_width + offset
            for target in range(seq_count)
            for offset in range(stretch_filters)
        ]
    )
    routed_taps = filter_taps[:, tap_columns].reshape(block_rows, seq_count, stretch_filters)
    packed = jnp.concatenate(
        [
            gated_grad.reshape(block_rows, seq_count, stretch_width),
            cached_input.reshape(block_rows, seq_count, stretch_width),
            routed_taps,
        ],
        axis=2,
    )
    moved = lax.all_to_all(packed, "seq", split_axis=1, concat_axis=0, tiled=True)
    moved = moved.reshape(length, 2 * stretch_width + stretch_filters)
    moved_grad = moved[:, :stretch_width]
    moved_input = moved[:, stretch_width : 2 * stretch_width]
    stretch_taps = moved[:, 2 * stretch_width :]
    shaped_grad = moved_grad.reshape(seq_count, block_rows, stretch_filters, stretch_group)
    blocks = jnp.pad(shaped_grad, ((0, seq_count - 1 + lag_group), (0, 0), (0, 0), (0, 0)))
    sources = moved_input.reshape(seq_count, block_rows, stretch_filters, stretch_group)
    trip_count = (seq_count + lag_group - 1) // lag_group
    input_acc, lag_acc = lag_sweep(
        blocks,
        0,
        seq_count,
        sources,
        lag_table(stretch_taps, block_rows),
        block_rows,
        trip_count,
        seq_count,
    )
    stretch_gain = lax.dynamic_slice_in_dim(skip_gain, seq_index * stretch_width, stretch_width, 0)
    conv_grad = input_acc.reshape(length, stretch_width) * taps_scale
    local_grad = (conv_grad + stretch_gain[None, :] * moved_grad.astype(jnp.float32)).astype(
        jnp.bfloat16
    )
    input_grad = lax.all_to_all(local_grad, "seq", split_axis=0, concat_axis=1, tiled=True)
    stretch_term = jnp.transpose(lag_acc[:, block_rows : block_rows + length]) * taps_scale
    lag_parts = lax.all_to_all(
        stretch_term.reshape(seq_count, block_rows, stretch_filters),
        "seq",
        split_axis=0,
        concat_axis=0,
        tiled=True,
    )
    sharers = seq_count * stretch_filters // filters
    filter_grad = (
        jnp.transpose(lag_parts, (1, 0, 2)).reshape(block_rows, filters, sharers).sum(axis=2)
    )
    return (input_grad, filter_grad)


def solution(mesh):
    return jax.shard_map(
        per_device,
        mesh=mesh,
        in_specs=(
            P(("groups", "seq"), "chan"),
            P(("groups", "seq"), "chan"),
            P(("groups", "seq"), "chan"),
            P("seq", "chan"),
            P("chan"),
        ),
        out_specs=(P(("groups", "seq"), "chan"), P(("groups", "seq"), "chan")),
        check_vma=False,
    )
```

profile of v0, /device:TPU:0, one launch (start us, length us, event | category | flops | bytes accessed | tf_op | source)
XLA Modules:
  0.0 98.7 jit_solution(5453652676311803673)
XLA Ops:
  0.7 1.4 %copy.32 = bf16[128,2048]{0,1:T(8,128)(2,1)S(1)} copy(bf16[128,2048]{1,0:T(8,128)(2,1)} %param.9) | data formatting | bytes 1048576 | tf_op args[0]
  2.1 0.1 multiply_convert_fusion
  2.2 0.3 copy.31
  2.5 0.6 gather_fusion
  3.1 1.1 %pad_maximum_fusion.4 = bf16[128,8,514]{0,2,1:T(8,128)(2,1)} fusion(bf16[128,8,2]{0,2,1:T(2,128)(2,1)S(1)} %bitcast.138, bf16[128,8,256]{0,2,1:T(8,128)(2,1)S(1)} %bitcast.136, bf16[128,8,256]{0,2,1:T(8,128)(2,1)S(1)} %bitcast.137), kind=kLoop, calls=%fused_computation.25 | loop fusion | flops 3158016 | bytes 2105344 | tf_op jit(solution)/shard_map/concatenate | solution.py:113
  4.2 7.3 %all-to-all-start = ((bf16[128,8,514]{0,2,1:T(8,128)(2,1)}), bf16[128,8,514]{0,2,1:T(8,128)(2,1)S(1)}, u32[]{:S(2)}, u32[]{:S(2)}) async-start(bf16[128,8,514]{0,2,1:T(8,128)(2,1)} %pad_maximum_fusion.4), calls=%async_computation | async-start | bytes 2129920 | tf_op jit(solution)/shard_map/all_to_all | solution.py:121
  11.4 0.8 dynamic_slice.63
  12.2 25.4 %all-to-all-done = bf16[128,8,514]{0,2,1:T(8,128)(2,1)S(1)} async-done(((bf16[128,8,514]{0,2,1:T(8,128)(2,1)}), bf16[128,8,514]{0,2,1:T(8,128)(2,1)S(1)}, u32[]{:S(2)}, u32[]{:S(2)}) %all-to-all-start) | async-done | bytes 1052704 | tf_op jit(solution)/shard_map/all_to_all | solution.py:121
  37.6 0.1 copy.63
  37.8 0.3 copy.51
  38.3 0.8 copy-done.3
  39.2 0.2 pad.52
  39.5 1.1 %copy.35 = bf16[8,128,2,128]{3,1,0,2:T(8,128)(2,1)} copy(bf16[8,128,2,128]{1,0,3,2:T(8,128)(2,1)S(1)} %bitcast.135) | data formatting | bytes 1048576
  40.6 26.8 %while.18 = (s32[]{:T(128)}, f32[8,128,2,128]{1,3,0,2:T(8,128)}, f32[2,1664]{1,0:T(2,128)S(1)}, bf16[19,128,2,128]{1,3,0,2:T(8,128)(2,1)S(1)}, bf16[2,1664]{1,0:...) while((s32[]{:T(128)}, f32[8,128,2,128]{1,3,0,2:T(8,128)}, ...), condition=%wide.region_2.3_spmd.clone, body=%wide.region_0.2_spmd.clone.sunk | while | flops 543954432 | bytes 31783416 | solution.py:86
  40.6 1.2 %dynamic-slice_bitcast_fusion.5 = (bf16[8,1,128,2,128]{2,4,1,0,3:T(8,128)(2,1)S(1)}, bf16[8,1,128,2,128]{2,4,1,0,3:T(8,128)(2,1)S(1)}, bf16[8,1,128,2,128]{2,4,1,0,3:T(8,128)(2,1)}, bf16[8,1,128,2,128]{2,4,1,0,3:T(8,128)(2,1)}) fusion(bf16[19,128,2,128]{1,3,0,2:T(8,128)(2,1)S(1)} %get-tuple-element.324, s32[]{:T(128)S(6)} %select_n.70, ...), kind=kLoop, calls=%fused_computation.9.clone.1 | loop fusion | bytes 4194320 | tf_op jit(solution)/shard_map/while/body/eval_jaxpr/stack | solution.py:49
  41.8 0.2 rev.24
  42.1 0.1 tile.29
  42.2 0.4 slice.144
  42.6 1.6 %reshape.107 = bf16[4,2,128,255]{3,2,1,0:T(8,128)(2,1)S(1)} reshape(bf16[4,2,32640]{2,1,0:T(2,128)(2,1)S(1)} %slice.144) | data formatting | bytes 1044480 | tf_op jit(solution)/shard_map/while/body/eval_jaxpr/reshape | solution.py:15
  44.2 3.1 %fusion.21 = f32[8,128,2,128]{1,3,0,2:T(8,128)} fusion(f32[8,128,2,128]{1,3,0,2:T(8,128)} %get-tuple-element.301, pred[]{:T(512)S(6)} %compare.9, bf16[8,1,128,2,128]{2,4,1,0,3:T(8,128)(2,1)S(1)} %get-tuple-element.269, bf16[8,1,128,2,128]{2,4,1,0,3:T(8,128)(2,1)} %get-tuple-element.270, bf16[8,1,128,2,128]{2,4,1,0,3:T(8,128)(2,1)} %get-tuple-element.271, ...), kind=kOutput, calls=%fused_computation.3.clone.1 | convolution fusion | flops 272105472 | bytes 4456449 | tf_op jit(solution)/shard_map/while/body/eval_jaxpr/kfts,iktfg->isfg/dot_general | solution.py:67
  47.3 1.1 %convolution_bitcast_fusion.3 = f32[4,2,128,128]{3,2,0,1:T(8,128)S(1)} fusion(bf16[8,128,2,128]{3,1,0,2:T(8,128)(2,1)S(1)} %copy-done.6, bf16[8,1,128,2,128]{2,4,1,0,3:T(8,128)(2,1)S(1)} %get-tuple-element.269, bf16[8,1,128,2,128]{2,4,1,0,3:T(8,128)(2,1)S(1)} %copy-done.1, bf16[8,1,128,2,128]{2,4,1,0,3:T(8,128)(2,1)S(1)} %copy-done.2, ...), kind=kOutput, calls=%fused_computation.4.clone.1 | convolution fusion | flops 271581184 | bytes 3145728 | tf_op jit(solution)/shard_map/while/body/eval_jaxpr/iktfg,isfg->kfts/dot_general | solution.py:70
  48.4 0.7 rev.25
  49.1 0.1 pad.125
  49.3 0.5 reshape.108
  49.8 1.0 %slice.145 = f32[4,2,32640]{2,0,1:T(4,128)} slice(f32[4,2,32768]{2,0,1:T(4,128)S(1)} %reshape.108), slice={[0:4], [0:2], [0:32640]} | slice | bytes 2088960 | tf_op jit(solution)/shard_map/while/body/eval_jaxpr/slice | solution.py:23
  50.8 2.8 %reshape.109 = f32[4,2,128,255]{3,2,0,1:T(8,128)S(1)} reshape(f32[4,2,32640]{2,0,1:T(4,128)} %slice.145) | data formatting | bytes 2088960 | tf_op jit(solution)/shard_map/while/body/eval_jaxpr/reshape | solution.py:24
  53.9 1.2 %dynamic-slice_bitcast_fusion.5 = (bf16[8,1,128,2,128]{2,4,1,0,3:T(8,128)(2,1)S(1)}, bf16[8,1,128,2,128]{2,4,1,0,3:T(8,128)(2,1)S(1)}, bf16[8,1,128,2,128]{2,4,1,0,3:T(8,128)(2,1)}, bf16[8,1,128,2,128]{2,4,1,0,3:T(8,128)(2,1)}) fusion(bf16[19,128,2,128]{1,3,0,2:T(8,128)(2,1)S(1)} %get-tuple-element.324, s32[]{:T(128)S(6)} %select_n.70, ...), kind=kLoop, calls=%fused_computation.9.clone.1 | loop fusion | bytes 4194320 | tf_op jit(solution)/shard_map/while/body/eval_jaxpr/stack | solution.py:49
  55.1 0.2 rev.24
  55.3 0.1 tile.29
  55.5 0.4 slice.144
  55.8 1.6 %reshape.107 = bf16[4,2,128,255]{3,2,1,0:T(8,128)(2,1)S(1)} reshape(bf16[4,2,32640]{2,1,0:T(2,128)(2,1)S(1)} %slice.144) | data formatting | bytes 1044480 | tf_op jit(solution)/shard_map/while/body/eval_jaxpr/reshape | solution.py:15
  57.4 3.5 %fusion.21 = f32[8,128,2,128]{1,3,0,2:T(8,128)} fusion(f32[8,128,2,128]{1,3,0,2:T(8,128)} %get-tuple-element.301, pred[]{:T(512)S(6)} %compare.9, bf16[8,1,128,2,128]{2,4,1,0,3:T(8,128)(2,1)S(1)} %get-tuple-element.269, bf16[8,1,128,2,128]{2,4,1,0,3:T(8,128)(2,1)} %get-tuple-element.270, bf16[8,1,128,2,128]{2,4,1,0,3:T(8,128)(2,1)} %get-tuple-element.271, ...), kind=kOutput, calls=%fused_computation.3.clone.1 | convolution fusion | flops 272105472 | bytes 4456449 | tf_op jit(solution)/shard_map/while/body/eval_jaxpr/kfts,iktfg->isfg/dot_general | solution.py:67
  60.9 1.1 %convolution_bitcast_fusion.3 = f32[4,2,128,128]{3,2,0,1:T(8,128)S(1)} fusion(bf16[8,128,2,128]{3,1,0,2:T(8,128)(2,1)S(1)} %copy-done.6, bf16[8,1,128,2,128]{2,4,1,0,3:T(8,128)(2,1)S(1)} %get-tuple-element.269, bf16[8,1,128,2,128]{2,4,1,0,3:T(8,128)(2,1)S(1)} %copy-done.1, bf16[8,1,128,2,128]{2,4,1,0,3:T(8,128)(2,1)S(1)} %copy-done.2, ...), kind=kOutput, calls=%fused_computation.4.clone.1 | convolution fusion | flops 271581184 | bytes 3145728 | tf_op jit(solution)/shard_map/while/body/eval_jaxpr/iktfg,isfg->kfts/dot_general | solution.py:70
  62.0 0.7 rev.25
  62.8 0.1 pad.125
  62.9 0.5 reshape.108
  63.4 1.0 %slice.145 = f32[4,2,32640]{2,0,1:T(4,128)} slice(f32[4,2,32768]{2,0,1:T(4,128)S(1)} %reshape.108), slice={[0:4], [0:2], [0:32640]} | slice | bytes 2088960 | tf_op jit(solution)/shard_map/while/body/eval_jaxpr/slice | solution.py:23
  64.4 2.8 %reshape.109 = f32[4,2,128,255]{3,2,0,1:T(8,128)S(1)} reshape(f32[4,2,32640]{2,0,1:T(4,128)} %slice.145) | data formatting | bytes 2088960 | tf_op jit(solution)/shard_map/while/body/eval_jaxpr/reshape | solution.py:24
  67.5 1.3 %broadcast_multiply_fusion = f32[8,128,2,128]{1,3,0,2:T(8,128)S(1)} fusion(f32[8,128,2,128]{1,3,0,2:T(8,128)} %get-tuple-element.161), kind=kLoop, calls=%fused_computation.33 | loop fusion | flops 262144 | bytes 2097152 | tf_op jit(solution)/shard_map/mul | solution.py:141
  68.8 0.6 copy.36
  69.4 0.6 multiply_bitcast_fusion
  70.0 3.6 %all-to-all-start.2 = ((f32[8,128,2]{1,2,0:T(2,128)}), f32[8,128,2]{1,2,0:T(2,128)S(1)}, u32[]{:S(2)}, u32[]{:S(2)}) async-start(f32[8,128,2]{1,2,0:T(2,128)} %multiply_bitcast_fusion), calls=%async_computation.2 | async-start | bytes 16384 | tf_op jit(solution)/shard_map/all_to_all | solution.py:147
  73.6 2.1 %copy_bitcast_fusion.3 = bf16[8,128,256]{1,2,0:T(8,128)(2,1)} fusion(f32[32,8,8,128]{3,2,1,0:T(8,128)S(1)} %bitcast.132, f32[256]{0:T(256)S(1)} %dynamic_slice.63, bf16[1024,514]{0,1:T(8,128)(2,1)} %bitcast.128), kind=kLoop, calls=%fused_computation.31 | loop fusion | flops 1048576 | bytes 2098176 | tf_op jit(solution)/shard_map/all_to_all | solution.py:145
  75.7 4.4 %all-to-all-done.2 = f32[8,128,2]{1,2,0:T(2,128)S(1)} async-done(((f32[8,128,2]{1,2,0:T(2,128)}), f32[8,128,2]{1,2,0:T(2,128)S(1)}, u32[]{:S(2)}, u32[]{:S(2)}) %all-to-all-start.2) | async-done | bytes 8224 | tf_op jit(solution)/shard_map/all_to_all | solution.py:147
  80.1 3.5 %all-to-all-start.1 = ((bf16[8,128,256]{1,2,0:T(8,128)(2,1)}), bf16[8,128,256]{1,2,0:T(8,128)(2,1)S(1)}, u32[]{:S(2)}, u32[]{:S(2)}) async-start(bf16[8,128,256]{1,2,0:T(8,128)(2,1)} %copy_bitcast_fusion.3), calls=%async_computation.1 | async-start | bytes 1048576 | tf_op jit(solution)/shard_map/all_to_all | solution.py:145
  83.6 13.4 %all-to-all-done.1 = bf16[8,128,256]{1,2,0:T(8,128)(2,1)S(1)} async-done(((bf16[8,128,256]{1,2,0:T(8,128)(2,1)}), bf16[8,128,256]{1,2,0:T(8,128)(2,1)S(1)}, u32[]{:S(2)}, u32[]{:S(2)}) %all-to-all-start.1) | async-done | bytes 524320 | tf_op jit(solution)/shard_map/all_to_all | solution.py:145
  97.1 1.0 %copy.39 = bf16[128,2048]{1,0:T(8,128)(2,1)} copy(bf16[128,2048]{0,1:T(8,128)(2,1)S(1)} %bitcast.133) | data formatting | bytes 1048576
  98.1 0.6 copy.79
  (44 shorter events, 1.0 us)
Async XLA Ops:
  0.6 1.9 %copy-start = (bf16[128,16]{0,1:T(8,128)(2,1)S(1)}, bf16[128,16]{0,1:T(8,128)(2,1)}, u32[]{:S(2)}) copy-start(bf16[128,16]{0,1:T(8,128)(2,1)} %param.12) | copy-start | bytes 12292
  0.6 1.4 %copy-start.4 = (bf16[128,2048]{1,0:T(8,128)(2,1)S(1)}, bf16[128,2048]{1,0:T(8,128)(2,1)}, u32[]{:S(2)}) copy-start(bf16[128,2048]{1,0:T(8,128)(2,1)} %param.10) | copy-start | bytes 1572868
  0.7 1.4 %copy-start.5 = (bf16[128,2048]{1,0:T(8,128)(2,1)S(1)}, bf16[128,2048]{1,0:T(8,128)(2,1)}, u32[]{:S(2)}) copy-start(bf16[128,2048]{1,0:T(8,128)(2,1)} %param.11) | copy-start | bytes 1572868
  4.2 33.4 %all-to-all-start = ((bf16[128,8,514]{0,2,1:T(8,128)(2,1)}), bf16[128,8,514]{0,2,1:T(8,128)(2,1)S(1)}, u32[]{:S(2)}, u32[]{:S(2)}) async-start(bf16[128,8,514]{0,2,1:T(8,128)(2,1)} %pad_maximum_fusion.4), calls=%async_computation | async-start | bytes 2129920 | tf_op jit(solution)/shard_map/all_to_all | solution.py:121
  38.1 1.0 copy-start.3
  44.1 3.2 %copy-start.1 = (bf16[8,1,128,2,128]{2,4,1,0,3:T(8,128)(2,1)S(1)}, bf16[8,1,128,2,128]{2,4,1,0,3:T(8,128)(2,1)}, u32[]{:S(2)}) copy-start(bf16[8,1,128,2,128]{2,4,1,0,3:T(8,128)(2,1)} %get-tuple-element.270) | copy-start | bytes 1572868 | tf_op jit(solution)/shard_map/while
  44.1 3.2 %copy-start.2 = (bf16[8,1,128,2,128]{2,4,1,0,3:T(8,128)(2,1)S(1)}, bf16[8,1,128,2,128]{2,4,1,0,3:T(8,128)(2,1)}, u32[]{:S(2)}) copy-start(bf16[8,1,128,2,128]{2,4,1,0,3:T(8,128)(2,1)} %get-tuple-element.271) | copy-start | bytes 1572868 | tf_op jit(solution)/shard_map/while
  44.2 3.1 %copy-start.6 = (bf16[8,128,2,128]{3,1,0,2:T(8,128)(2,1)S(1)}, bf16[8,128,2,128]{3,1,0,2:T(8,128)(2,1)}, u32[]{:S(2)}) copy-start(bf16[8,128,2,128]{3,1,0,2:T(8,128)(2,1)} %get-tuple-element.326) | copy-start | bytes 1572868 | tf_op jit(solution)/shard_map/while
  57.4 3.5 %copy-start.1 = (bf16[8,1,128,2,128]{2,4,1,0,3:T(8,128)(2,1)S(1)}, bf16[8,1,128,2,128]{2,4,1,0,3:T(8,128)(2,1)}, u32[]{:S(2)}) copy-start(bf16[8,1,128,2,128]{2,4,1,0,3:T(8,128)(2,1)} %get-tuple-element.270) | copy-start | bytes 1572868 | tf_op jit(solution)/shard_map/while
  57.4 3.5 %copy-start.2 = (bf16[8,1,128,2,128]{2,4,1,0,3:T(8,128)(2,1)S(1)}, bf16[8,1,128,2,128]{2,4,1,0,3:T(8,128)(2,1)}, u32[]{:S(2)}) copy-start(bf16[8,1,128,2,128]{2,4,1,0,3:T(8,128)(2,1)} %get-tuple-element.271) | copy-start | bytes 1572868 | tf_op jit(solution)/shard_map/while
  57.4 3.5 %copy-start.6 = (bf16[8,128,2,128]{3,1,0,2:T(8,128)(2,1)S(1)}, bf16[8,128,2,128]{3,1,0,2:T(8,128)(2,1)}, u32[]{:S(2)}) copy-start(bf16[8,128,2,128]{3,1,0,2:T(8,128)(2,1)} %get-tuple-element.326) | copy-start | bytes 1572868 | tf_op jit(solution)/shard_map/while
  70.0 10.1 %all-to-all-start.2 = ((f32[8,128,2]{1,2,0:T(2,128)}), f32[8,128,2]{1,2,0:T(2,128)S(1)}, u32[]{:S(2)}, u32[]{:S(2)}) async-start(f32[8,128,2]{1,2,0:T(2,128)} %multiply_bitcast_fusion), calls=%async_computation.2 | async-start | bytes 16384 | tf_op jit(solution)/shard_map/all_to_all | solution.py:147
  80.1 16.9 %all-to-all-start.1 = ((bf16[8,128,256]{1,2,0:T(8,128)(2,1)}), bf16[8,128,256]{1,2,0:T(8,128)(2,1)S(1)}, u32[]{:S(2)}, u32[]{:S(2)}) async-start(bf16[8,128,256]{1,2,0:T(8,128)(2,1)} %copy_bitcast_fusion.3), calls=%async_computation.1 | async-start | bytes 1048576 | tf_op jit(solution)/shard_map/all_to_all | solution.py:145
where the time goes:
time: 99.2 us; the launch traced here: 98.7 us
  waiting for transfers between devices  43.2 us (44%)
  local copies, waits for them, and re-layouts  25.7 us (26%)
  starting transfers between devices  14.4 us (15%)
  matrix products  8.83 us (9%)
  other arithmetic  5.49 us (6%)
    all_to_all x1, waiting for transfers between devices, per_device(): lax.all_to_all(packed, 'seq', split_axis=1, concat_axis=0, tiled=True)  25.4 us
    all_to_all x1, waiting for transfers between devices, per_device(): lax.all_to_all(local_grad, 'seq', split_axis=0, concat_axis=1, tiled=True)  13.4 us
    all_to_all x1, starting transfers between devices, per_device(): lax.all_to_all(packed, 'seq', split_axis=1, concat_axis=0, tiled=True)  7.28 us
    dot_general x2, matrix products, advance(): jnp.einsum('kfts,iktfg->isfg', toeplitz, stacked, preferred_element_type=...  6.6 us
    reshape x2, local copies, waits for them, and re-layouts, diagonal_sums(): trimmed.reshape(products.shape[0], products.shape[1], block_rows, 2 * blo...  5.62 us
    unnamed x17, local copies, waits for them, and re-layouts  5.54 us
    all_to_all x1, waiting for transfers between devices, per_device(): lax.all_to_all(stretch_term.reshape(seq_count, block_rows, stretch_filter...  4.37 us
    all_to_all x1, starting transfers between devices, per_device(): lax.all_to_all(stretch_term.reshape(seq_count, block_rows, stretch_filter...  3.59 us
  transfers between devices with their start and end apart: 3, of which 3 were waited for; matrix products, arithmetic and copies ran while one was open for 3% of the time, Pallas kernels for 0%

commit v1 on v0

--- a/solution.py
+++ b/solution.py
@@ -142,7 +142,9 @@
     local_grad = (conv_grad + stretch_gain[None, :] * moved_grad.astype(jnp.float32)).astype(
         jnp.bfloat16
     )
-    input_grad = lax.all_to_all(local_grad, "seq", split_axis=0, concat_axis=1, tiled=True)
+    parts = jnp.split(local_grad, lax.axis_size("seq"), axis=0)
+    received = lax.all_to_all(jnp.stack(parts), "seq", 0, 0)
+    input_grad = jnp.concatenate(received, axis=1)
     stretch_term = jnp.transpose(lag_acc[:, block_rows : block_rows + length]) * taps_scale
     lag_parts = lax.all_to_all(
         stretch_term.reshape(seq_count, block_rows, stretch_filters),

time: 99.2 us -> 105 us (1.058)
  local copies, waits for them, and re-layouts: 25.7 us -> 30.9 us
  waiting for transfers between devices: 43.2 us -> 44.7 us
    unnamed x17 -> x24, local copies, waits for them, and re-layouts: 5.54 us -> 10.1 us
    all_to_all x1 -> x0, other arithmetic: 2.14 us -> none  [per_device(): lax.all_to_all(local_grad, 'seq', split_axis=0, concat_axis=1, tiled=True)]
    all_to_all x1, waiting for transfers between devices: 4.37 us -> 5.87 us  [per_device(): lax.all_to_all(stretch_term.reshape(seq_count, block_rows, stretch_filter...]
    convert_element_type x0 -> x1, other arithmetic: none -> 1.32 us  [per_device(): (conv_grad + stretch_gain[None, :] * moved_grad.astype(jnp.float32)).asty...]
  transfers between devices with their start and end apart: 3 -> 3, of which waited for: 3 -> 3; matrix products, arithmetic and copies ran while one was open for 3% -> 1% of each run, Pallas kernels for 0% -> 0%
where the time goes in v1:
time: 105 us
  waiting for transfers between devices  44.7 us (43%)
  local copies, waits for them, and re-layouts  30.9 us (29%)
  starting transfers between devices  14.4 us (14%)
  matrix products  8.83 us (8%)
  other arithmetic  4.66 us (4%)
    all_to_all x1, waiting for transfers between devices, per_device(): lax.all_to_all(packed, 'seq', split_axis=1, concat_axis=0, tiled=True)  25.4 us
    all_to_all x1, waiting for transfers between devices, per_device(): received = lax.all_to_all(jnp.stack(parts), 'seq', 0, 0)  13.4 us
    unnamed x24, local copies, waits for them, and re-layouts  10.1 us
    all_to_all x1, starting transfers between devices, per_device(): lax.all_to_all(packed, 'seq', split_axis=1, concat_axis=0, tiled=True)  7.28 us
    dot_general x2, matrix products, advance(): jnp.einsum('kfts,iktfg->isfg', toeplitz, stacked, preferred_element_type=...  6.6 us
    all_to_all x1, waiting for transfers between devices, per_device(): lax.all_to_all(stretch_term.reshape(seq_count, block_rows, stretch_filter...  5.87 us
    reshape x2, local copies, waits for them, and re-layouts, diagonal_sums(): trimmed.reshape(products.shape[0], products.shape[1], block_rows, 2 * blo...  5.62 us
    all_to_all x1, starting transfers between devices, per_device(): lax.all_to_all(stretch_term.reshape(seq_count, block_rows, stretch_filter...  3.59 us
  transfers between devices with their start and end apart: 3, of which 3 were waited for; matrix products, arithmetic and copies ran while one was open for 1% of the time, Pallas kernels for 0%

profile of v1, /device:TPU:0, one launch (start us, length us, event | category | flops | bytes accessed | tf_op | source)
XLA Modules:
  0.0 104.5 jit_solution(15542149275491190775)
XLA Ops:
  0.7 1.4 %copy.32 = bf16[128,2048]{0,1:T(8,128)(2,1)S(1)} copy(bf16[128,2048]{1,0:T(8,128)(2,1)} %param.9) | data formatting | bytes 1048576 | tf_op args[0]
  2.2 0.3 copy.31
  2.5 0.6 gather_fusion
  3.1 1.1 %pad_maximum_fusion.4 = bf16[128,8,514]{0,2,1:T(8,128)(2,1)} fusion(bf16[128,8,2]{0,2,1:T(2,128)(2,1)S(1)} %bitcast.162, bf16[128,8,256]{0,2,1:T(8,128)(2,1)S(1)} %bitcast.160, bf16[128,8,256]{0,2,1:T(8,128)(2,1)S(1)} %bitcast.161), kind=kLoop, calls=%fused_computation.25 | loop fusion | flops 3158016 | bytes 2105344 | tf_op jit(solution)/shard_map/concatenate | solution.py:113
  4.2 7.3 %all-to-all-start = ((bf16[128,8,514]{0,2,1:T(8,128)(2,1)}), bf16[128,8,514]{0,2,1:T(8,128)(2,1)S(1)}, u32[]{:S(2)}, u32[]{:S(2)}) async-start(bf16[128,8,514]{0,2,1:T(8,128)(2,1)} %pad_maximum_fusion.4), calls=%async_computation | async-start | bytes 2129920 | tf_op jit(solution)/shard_map/all_to_all | solution.py:121
  11.4 0.8 dynamic_slice.63
  12.2 25.4 %all-to-all-done = bf16[128,8,514]{0,2,1:T(8,128)(2,1)S(1)} async-done(((bf16[128,8,514]{0,2,1:T(8,128)(2,1)}), bf16[128,8,514]{0,2,1:T(8,128)(2,1)S(1)}, u32[]{:S(2)}, u32[]{:S(2)}) %all-to-all-start) | async-done | bytes 1052704 | tf_op jit(solution)/shard_map/all_to_all | solution.py:121
  37.8 0.3 copy.49
  38.3 0.8 copy-done.3
  39.1 0.2 pad.52
  39.5 1.1 %copy.35 = bf16[8,128,2,128]{3,1,0,2:T(8,128)(2,1)} copy(bf16[8,128,2,128]{1,0,3,2:T(8,128)(2,1)S(1)} %bitcast.159) | data formatting | bytes 1048576
  40.6 26.8 %while.18 = (s32[]{:T(128)}, f32[8,128,2,128]{1,3,0,2:T(8,128)}, f32[2,1664]{1,0:T(2,128)S(1)}, bf16[19,128,2,128]{1,3,0,2:T(8,128)(2,1)S(1)}, bf16[2,1664]{1,0:...) while((s32[]{:T(128)}, f32[8,128,2,128]{1,3,0,2:T(8,128)}, ...), condition=%wide.region_2.3_spmd.clone, body=%wide.region_0.2_spmd.clone.sunk | while | flops 543954432 | bytes 31783416 | solution.py:86
  40.6 1.2 %dynamic-slice_bitcast_fusion.5 = (bf16[8,1,128,2,128]{2,4,1,0,3:T(8,128)(2,1)S(1)}, bf16[8,1,128,2,128]{2,4,1,0,3:T(8,128)(2,1)S(1)}, bf16[8,1,128,2,128]{2,4,1,0,3:T(8,128)(2,1)}, bf16[8,1,128,2,128]{2,4,1,0,3:T(8,128)(2,1)}) fusion(bf16[19,128,2,128]{1,3,0,2:T(8,128)(2,1)S(1)} %get-tuple-element.326, s32[]{:T(128)S(6)} %select_n.70, ...), kind=kLoop, calls=%fused_computation.9.clone.1 | loop fusion | bytes 4194320 | tf_op jit(solution)/shard_map/while/body/eval_jaxpr/stack | solution.py:49
  42.2 0.4 slice.143
  42.6 1.6 %reshape.112 = bf16[4,2,128,255]{3,2,1,0:T(8,128)(2,1)S(1)} reshape(bf16[4,2,32640]{2,1,0:T(2,128)(2,1)S(1)} %slice.143) | data formatting | bytes 1044480 | tf_op jit(solution)/shard_map/while/body/eval_jaxpr/reshape | solution.py:15
  44.2 3.1 %fusion.27 = f32[8,128,2,128]{1,3,0,2:T(8,128)} fusion(f32[8,128,2,128]{1,3,0,2:T(8,128)} %get-tuple-element.303, pred[]{:T(512)S(6)} %compare.9, bf16[8,1,128,2,128]{2,4,1,0,3:T(8,128)(2,1)S(1)} %get-tuple-element.271, bf16[8,1,128,2,128]{2,4,1,0,3:T(8,128)(2,1)} %get-tuple-element.272, bf16[8,1,128,2,128]{2,4,1,0,3:T(8,128)(2,1)} %get-tuple-element.273, ...), kind=kOutput, calls=%fused_computation.3.clone.1 | convolution fusion | flops 272105472 | bytes 4456449 | tf_op jit(solution)/shard_map/while/body/eval_jaxpr/kfts,iktfg->isfg/dot_general | solution.py:67
  47.3 1.1 %convolution_bitcast_fusion.3 = f32[4,2,128,128]{3,2,0,1:T(8,128)S(1)} fusion(bf16[8,128,2,128]{3,1,0,2:T(8,128)(2,1)S(1)} %copy-done.6, bf16[8,1,128,2,128]{2,4,1,0,3:T(8,128)(2,1)S(1)} %get-tuple-element.271, bf16[8,1,128,2,128]{2,4,1,0,3:T(8,128)(2,1)S(1)} %copy-done.1, bf16[8,1,128,2,128]{2,4,1,0,3:T(8,128)(2,1)S(1)} %copy-done.2, ...), kind=kOutput, calls=%fused_computation.4.clone.1 | convolution fusion | flops 271581184 | bytes 3145728 | tf_op jit(solution)/shard_map/while/body/eval_jaxpr/iktfg,isfg->kfts/dot_general | solution.py:70
  48.4 0.7 rev.25
  49.3 0.5 reshape.113
  49.8 1.0 slice.144
  50.8 2.8 %reshape.114 = f32[4,2,128,255]{3,2,0,1:T(8,128)S(1)} reshape(f32[4,2,32640]{2,0,1:T(4,128)} %slice.144) | data formatting | bytes 2088960 | tf_op jit(solution)/shard_map/while/body/eval_jaxpr/reshape | solution.py:24
  53.9 1.2 %dynamic-slice_bitcast_fusion.5 = (bf16[8,1,128,2,128]{2,4,1,0,3:T(8,128)(2,1)S(1)}, bf16[8,1,128,2,128]{2,4,1,0,3:T(8,128)(2,1)S(1)}, bf16[8,1,128,2,128]{2,4,1,0,3:T(8,128)(2,1)}, bf16[8,1,128,2,128]{2,4,1,0,3:T(8,128)(2,1)}) fusion(bf16[19,128,2,128]{1,3,0,2:T(8,128)(2,1)S(1)} %get-tuple-element.326, s32[]{:T(128)S(6)} %select_n.70, ...), kind=kLoop, calls=%fused_computation.9.clone.1 | loop fusion | bytes 4194320 | tf_op jit(solution)/shard_map/while/body/eval_jaxpr/stack | solution.py:49
  55.5 0.4 slice.143
  55.8 1.6 %reshape.112 = bf16[4,2,128,255]{3,2,1,0:T(8,128)(2,1)S(1)} reshape(bf16[4,2,32640]{2,1,0:T(2,128)(2,1)S(1)} %slice.143) | data formatting | bytes 1044480 | tf_op jit(solution)/shard_map/while/body/eval_jaxpr/reshape | solution.py:15
  57.4 3.5 %fusion.27 = f32[8,128,2,128]{1,3,0,2:T(8,128)} fusion(f32[8,128,2,128]{1,3,0,2:T(8,128)} %get-tuple-element.303, pred[]{:T(512)S(6)} %compare.9, bf16[8,1,128,2,128]{2,4,1,0,3:T(8,128)(2,1)S(1)} %get-tuple-element.271, bf16[8,1,128,2,128]{2,4,1,0,3:T(8,128)(2,1)} %get-tuple-element.272, bf16[8,1,128,2,128]{2,4,1,0,3:T(8,128)(2,1)} %get-tuple-element.273, ...), kind=kOutput, calls=%fused_computation.3.clone.1 | convolution fusion | flops 272105472 | bytes 4456449 | tf_op jit(solution)/shard_map/while/body/eval_jaxpr/kfts,iktfg->isfg/dot_general | solution.py:67
  60.9 1.1 %convolution_bitcast_fusion.3 = f32[4,2,128,128]{3,2,0,1:T(8,128)S(1)} fusion(bf16[8,128,2,128]{3,1,0,2:T(8,128)(2,1)S(1)} %copy-done.6, bf16[8,1,128,2,128]{2,4,1,0,3:T(8,128)(2,1)S(1)} %get-tuple-element.271, bf16[8,1,128,2,128]{2,4,1,0,3:T(8,128)(2,1)S(1)} %copy-done.1, bf16[8,1,128,2,128]{2,4,1,0,3:T(8,128)(2,1)S(1)} %copy-done.2, ...), kind=kOutput, calls=%fused_computation.4.clone.1 | convolution fusion | flops 271581184 | bytes 3145728 | tf_op jit(solution)/shard_map/while/body/eval_jaxpr/iktfg,isfg->kfts/dot_general | solution.py:70
  62.0 0.7 rev.25
  62.9 0.5 reshape.113
  63.4 1.0 slice.144
  64.4 2.8 %reshape.114 = f32[4,2,128,255]{3,2,0,1:T(8,128)S(1)} reshape(f32[4,2,32640]{2,0,1:T(4,128)} %slice.144) | data formatting | bytes 2088960 | tf_op jit(solution)/shard_map/while/body/eval_jaxpr/reshape | solution.py:24
  67.5 1.3 %broadcast_multiply_fusion = f32[8,128,2,128]{1,3,0,2:T(8,128)S(1)} fusion(f32[8,128,2,128]{1,3,0,2:T(8,128)} %get-tuple-element.161), kind=kLoop, calls=%fused_computation.31 | loop fusion | flops 262144 | bytes 2097152 | tf_op jit(solution)/shard_map/mul | solution.py:141
  68.8 0.6 copy.36
  69.4 1.3 %fusion.9 = bf16[1024,256]{0,1:T(8,128)(2,1)S(1)} fusion(f32[32,8,8,128]{3,2,1,0:T(8,128)S(1)} %bitcast.156, f32[256]{0:T(256)S(1)} %dynamic_slice.63, bf16[1024,514]{0,1:T(8,128)(2,1)} %bitcast.152), kind=kLoop, calls=%fused_computation.28 | loop fusion | flops 1048576 | bytes 2098176 | tf_op jit(solution)/shard_map/convert_element_type | solution.py:142
  70.7 0.6 fusion.17
  71.4 0.6 fusion.16
  72.0 0.6 fusion.15
  72.7 0.6 fusion.14
  73.3 0.6 fusion.13
  74.0 0.6 fusion.12
  74.6 0.6 fusion.11
  75.3 0.6 multiply_bitcast_fusion
  75.9 3.6 %all-to-all-start.2 = ((f32[8,128,2]{1,2,0:T(2,128)}), f32[8,128,2]{1,2,0:T(2,128)S(1)}, u32[]{:S(2)}, u32[]{:S(2)}) async-start(f32[8,128,2]{1,2,0:T(2,128)} %multiply_bitcast_fusion), calls=%async_computation.2 | async-start | bytes 16384 | tf_op jit(solution)/shard_map/all_to_all | solution.py:149
  79.5 0.6 fusion.10
  80.1 5.9 %all-to-all-done.2 = f32[8,128,2]{1,2,0:T(2,128)S(1)} async-done(((f32[8,128,2]{1,2,0:T(2,128)}), f32[8,128,2]{1,2,0:T(2,128)S(1)}, u32[]{:S(2)}, u32[]{:S(2)}) %all-to-all-start.2) | async-done | bytes 8224 | tf_op jit(solution)/shard_map/all_to_all | solution.py:149
  86.0 3.5 %all-to-all-start.1 = ((bf16[8,128,256]{1,2,0:T(8,128)(2,1)}), bf16[8,128,256]{1,2,0:T(8,128)(2,1)S(1)}, u32[]{:S(2)}, u32[]{:S(2)}) async-start(bf16[8,128,256]{1,2,0:T(8,128)(2,1)} %fusion.10), calls=%async_computation.1 | async-start | bytes 1048576 | tf_op jit(solution)/shard_map/all_to_all | solution.py:146
  89.5 13.4 %all-to-all-done.1 = bf16[8,128,256]{1,2,0:T(8,128)(2,1)S(1)} async-done(((bf16[8,128,256]{1,2,0:T(8,128)(2,1)}), bf16[8,128,256]{1,2,0:T(8,128)(2,1)S(1)}, u32[]{:S(2)}, u32[]{:S(2)}) %all-to-all-start.1) | async-done | bytes 524320 | tf_op jit(solution)/shard_map/all_to_all | solution.py:146
  102.9 1.0 copy.38
  103.9 0.6 copy.80
  (52 shorter events, 2.1 us)
Async XLA Ops:
  0.6 1.9 %copy-start = (bf16[128,16]{0,1:T(8,128)(2,1)S(1)}, bf16[128,16]{0,1:T(8,128)(2,1)}, u32[]{:S(2)}) copy-start(bf16[128,16]{0,1:T(8,128)(2,1)} %param.12) | copy-start | bytes 12292
  0.6 1.4 %copy-start.4 = (bf16[128,2048]{1,0:T(8,128)(2,1)S(1)}, bf16[128,2048]{1,0:T(8,128)(2,1)}, u32[]{:S(2)}) copy-start(bf16[128,2048]{1,0:T(8,128)(2,1)} %param.10) | copy-start | bytes 1572868
  0.7 1.4 %copy-start.5 = (bf16[128,2048]{1,0:T(8,128)(2,1)S(1)}, bf16[128,2048]{1,0:T(8,128)(2,1)}, u32[]{:S(2)}) copy-start(bf16[128,2048]{1,0:T(8,128)(2,1)} %param.11) | copy-start | bytes 1572868
  4.2 33.4 %all-to-all-start = ((bf16[128,8,514]{0,2,1:T(8,128)(2,1)}), bf16[128,8,514]{0,2,1:T(8,128)(2,1)S(1)}, u32[]{:S(2)}, u32[]{:S(2)}) async-start(bf16[128,8,514]{0,2,1:T(8,128)(2,1)} %pad_maximum_fusion.4), calls=%async_computation | async-start | bytes 2129920 | tf_op jit(solution)/shard_map/all_to_all | solution.py:121
  38.1 1.0 copy-start.3
  44.1 3.2 %copy-start.1 = (bf16[8,1,128,2,128]{2,4,1,0,3:T(8,128)(2,1)S(1)}, bf16[8,1,128,2,128]{2,4,1,0,3:T(8,128)(2,1)}, u32[]{:S(2)}) copy-start(bf16[8,1,128,2,128]{2,4,1,0,3:T(8,128)(2,1)} %get-tuple-element.272) | copy-start | bytes 1572868 | tf_op jit(solution)/shard_map/while
  44.1 3.2 %copy-start.2 = (bf16[8,1,128,2,128]{2,4,1,0,3:T(8,128)(2,1)S(1)}, bf16[8,1,128,2,128]{2,4,1,0,3:T(8,128)(2,1)}, u32[]{:S(2)}) copy-start(bf16[8,1,128,2,128]{2,4,1,0,3:T(8,128)(2,1)} %get-tuple-element.273) | copy-start | bytes 1572868 | tf_op jit(solution)/shard_map/while
  44.2 3.1 %copy-start.6 = (bf16[8,128,2,128]{3,1,0,2:T(8,128)(2,1)S(1)}, bf16[8,128,2,128]{3,1,0,2:T(8,128)(2,1)}, u32[]{:S(2)}) copy-start(bf16[8,128,2,128]{3,1,0,2:T(8,128)(2,1)} %get-tuple-element.328) | copy-start | bytes 1572868 | tf_op jit(solution)/shard_map/while
  57.4 3.5 %copy-start.1 = (bf16[8,1,128,2,128]{2,4,1,0,3:T(8,128)(2,1)S(1)}, bf16[8,1,128,2,128]{2,4,1,0,3:T(8,128)(2,1)}, u32[]{:S(2)}) copy-start(bf16[8,1,128,2,128]{2,4,1,0,3:T(8,128)(2,1)} %get-tuple-element.272) | copy-start | bytes 1572868 | tf_op jit(solution)/shard_map/while
  57.4 3.5 %copy-start.2 = (bf16[8,1,128,2,128]{2,4,1,0,3:T(8,128)(2,1)S(1)}, bf16[8,1,128,2,128]{2,4,1,0,3:T(8,128)(2,1)}, u32[]{:S(2)}) copy-start(bf16[8,1,128,2,128]{2,4,1,0,3:T(8,128)(2,1)} %get-tuple-element.273) | copy-start | bytes 1572868 | tf_op jit(solution)/shard_map/while
  57.4 3.5 %copy-start.6 = (bf16[8,128,2,128]{3,1,0,2:T(8,128)(2,1)S(1)}, bf16[8,128,2,128]{3,1,0,2:T(8,128)(2,1)}, u32[]{:S(2)}) copy-start(bf16[8,128,2,128]{3,1,0,2:T(8,128)(2,1)} %get-tuple-element.328) | copy-start | bytes 1572868 | tf_op jit(solution)/shard_map/while
  75.9 10.1 %all-to-all-start.2 = ((f32[8,128,2]{1,2,0:T(2,128)}), f32[8,128,2]{1,2,0:T(2,128)S(1)}, u32[]{:S(2)}, u32[]{:S(2)}) async-start(f32[8,128,2]{1,2,0:T(2,128)} %multiply_bitcast_fusion), calls=%async_computation.2 | async-start | bytes 16384 | tf_op jit(solution)/shard_map/all_to_all | solution.py:149
  86.0 16.9 %all-to-all-start.1 = ((bf16[8,128,256]{1,2,0:T(8,128)(2,1)}), bf16[8,128,256]{1,2,0:T(8,128)(2,1)S(1)}, u32[]{:S(2)}, u32[]{:S(2)}) async-start(bf16[8,128,256]{1,2,0:T(8,128)(2,1)} %fusion.10), calls=%async_computation.1 | async-start | bytes 1048576 | tf_op jit(solution)/shard_map/all_to_all | solution.py:146
